TPU v7x, 512 devices: a whole 4x4x16 slice. The times are simulated.
512 devices in a mesh: dp: 16 (over z), expert: 32 (over x, y, core).
Axes of the slice: x: 4, y: 4, z: 16, core: 2. Of those that a mesh axis runs over, the one named last changes fastest.
Arguments:
- x_tokens: bfloat16 [65536, 2048], P(('dp', 'expert')), may hold values from -6 to 6
- grad_out: bfloat16 [65536, 2048], P(('dp', 'expert')), may hold values from -6 to 6
- expert_ids: int32 [65536, 2], P(('dp', 'expert')), may hold values from 0 to 31, all different within a row; in each aligned block of 128 rows (0 to 127, 128 to 255, ...) at most 10 rows name the same one
- route_probs: float32 [65536, 2], P(('dp', 'expert')), may hold values from 0.1 to 1
- w_gate: bfloat16 [32, 2048, 768], P('expert', 'dp'), may hold values from -0.125 to 0.125
- w_up: bfloat16 [32, 2048, 768], P('expert', 'dp'), may hold values from -0.125 to 0.125
- w_down: bfloat16 [32, 2048, 768], P('expert', 'dp'), may hold values from -0.21875 to 0.21875
Outputs:
- grad_x: bfloat16 [65536, 2048], P(('dp', 'expert'))
- grad_probs: bfloat16 [65536, 2], P(('dp', 'expert'))
- grad_w_down: bfloat16 [32, 2048, 768], P('expert', 'dp')
Inputs may be any that keep to these rules, and one draw needn't show every extreme that they name: `expert_ids`: each token names 2 different experts; among the 128 tokens of one device no expert is named by more than 10 routes, and in every draw some device names some expert exactly 10 times.
All inputs are finite; a program needn't handle non-finite values.
Results may differ from a plain program's by a relative error of at most 0.017.
Values may be sent and summed in bfloat16 or wider, within the bound.
No kernel may reach another device: no remote copies, remote signals or barrier semaphores. Data moves between devices by JAX's collectives and lax.ppermute only.
A program may use at most 64 MiB of HBM per device.

v0:
```python
import jax
import jax.numpy as jnp
from jax import lax
from jax.sharding import PartitionSpec as P


def per_device(x_tokens, grad_out, expert_ids, route_probs, w_gate, w_up, w_down):
    tok_count, model_width = x_tokens.shape
    top_count = expert_ids.shape[1]
    n_expert = lax.axis_size("expert")
    capacity = tok_count * top_count * 5 // (4 * n_expert)
    slot_count = n_expert * capacity
    routes = tok_count * top_count
    flat_ids = expert_ids.reshape(routes)
    onehot = (flat_ids[:, None] == jnp.arange(n_expert, dtype=jnp.int32)).astype(jnp.int32)
    route_rank = jnp.sum((jnp.cumsum(onehot, axis=0) - onehot) * onehot, axis=1)
    target = flat_ids * capacity + route_rank
    source = (
        jnp.full((slot_count,), routes, jnp.int32)
        .at[target]
        .set(jnp.arange(routes, dtype=jnp.int32))
    )
    token_of = jnp.where(source < routes, source // top_count, tok_count)
    x_padded = jnp.concatenate([x_tokens, jnp.zeros((1, model_width), jnp.bfloat16)], axis=0)
    dy_padded = jnp.concatenate([grad_out, jnp.zeros((1, model_width), jnp.bfloat16)], axis=0)
    p_padded = jnp.concatenate([route_probs.reshape(routes), jnp.zeros((1,), jnp.float32)]).astype(
        jnp.bfloat16
    )
    x_slots = x_padded[token_of].reshape(n_expert, capacity, model_width)
    dy_slots = dy_padded[token_of].reshape(n_expert, capacity, model_width)
    p_slots = p_padded[source].reshape(n_expert, capacity)
    arrived = (
        lax.all_to_all(x_slots, "expert", split_axis=0, concat_axis=0, tiled=True),
        lax.all_to_all(dy_slots, "expert", split_axis=0, concat_axis=0, tiled=True),
        lax.all_to_all(p_slots, "expert", split_axis=0, concat_axis=0, tiled=True),
    )
    in_rows = arrived[0].reshape(slot_count, model_width)
    dy_rows = arrived[1].reshape(slot_count, model_width)
    p_rows = arrived[2].reshape(slot_count).astype(jnp.float32)
    scaled = (p_rows[:, None] * dy_rows.astype(jnp.float32)).astype(jnp.bfloat16)
    gate_full, up_full = (
        lax.all_gather(w_gate, "dp", axis=1, tiled=True),
        lax.all_gather(w_up, "dp", axis=1, tiled=True),
    )
    gate_full = gate_full[0]
    up_full = up_full[0]
    gate_pre = jnp.dot(in_rows, gate_full, preferred_element_type=jnp.float32)
    up_pre = jnp.dot(in_rows, up_full, preferred_element_type=jnp.float32)
    gate_sig = jax.nn.sigmoid(gate_pre)
    gate_act = gate_pre * gate_sig
    hidden = (gate_act * up_pre).astype(jnp.bfloat16)
    piece_rows = lax.all_gather(w_down, "dp", axis=1, tiled=True)[0]
    out_piece = jnp.dot(hidden, piece_rows.T, preferred_element_type=jnp.float32)
    grad_sum = jnp.dot(scaled, piece_rows, preferred_element_type=jnp.float32)
    prob_sum = jnp.sum(dy_rows.astype(jnp.float32) * out_piece, axis=1)
    hidden_grad, prob_sum = (grad_sum, prob_sum)
    up_grad = (hidden_grad * gate_act).astype(jnp.bfloat16)
    gate_grad = (hidden_grad * up_pre * gate_sig * (1.0 + gate_pre * (1.0 - gate_sig))).astype(
        jnp.bfloat16
    )
    x_grad = (
        jnp.dot(gate_grad, gate_full.T, preferred_element_type=jnp.float32)
        + jnp.dot(up_grad, up_full.T, preferred_element_type=jnp.float32)
    ).astype(jnp.bfloat16)
    down_grad = lax.psum_scatter(
        lax.dot_general(
            scaled, hidden, (((0,), (0,)), ((), ())), preferred_element_type=jnp.float32
        ).astype(jnp.bfloat16),
        "dp",
        scatter_dimension=0,
        tiled=True,
    )
    grad_w_down = down_grad[None]
    returned = (
        lax.all_to_all(
            x_grad.reshape(n_expert, capacity, model_width),
            "expert",
            split_axis=0,
            concat_axis=0,
            tiled=True,
        ),
        lax.all_to_all(
            prob_sum.astype(jnp.bfloat16).reshape(n_expert, capacity),
            "expert",
            split_axis=0,
            concat_axis=0,
            tiled=True,
        ),
    )
    grad_slots = returned[0].reshape(slot_count, model_width)
    prob_slots = returned[1].reshape(slot_count)
    picked = grad_slots[target].astype(jnp.float32).reshape(tok_count, top_count, model_width)
    grad_x = jnp.sum(picked, axis=1).astype(jnp.bfloat16)
    grad_probs = prob_slots[target].reshape(tok_count, top_count)
    return (grad_x, grad_probs, grad_w_down)


def solution(mesh):
    return jax.shard_map(
        per_device,
        mesh=mesh,
        in_specs=(
            P(("dp", "expert"), None),
            P(("dp", "expert"), None),
            P(("dp", "expert"), None),
            P(("dp", "expert"), None),
            P("expert", "dp", None),
            P("expert", "dp", None),
            P("expert", "dp", None),
        ),
        out_specs=(P(("dp", "expert"), None), P(("dp", "expert"), None), P("expert", "dp", None)),
        check_vma=False,
    )
```

profile of v0, /device:TPU:4, one launch (start us, length us, event | category | flops | bytes accessed | tf_op | source)
XLA Modules:
  0.0 322.4 jit_solution(13100136976467206266)
XLA Ops:
  7.2 0.7 all-gather.8.cloned.1.call-update
  8.0 0.7 all-gather.6.cloned.1.call-update
  8.7 0.7 all-gather.4.cloned.1.call-update
  9.4 0.8 copy.18
  10.5 0.7 convert.9
  11.4 0.7 broadcast_multiply_fusion
  12.4 0.6 reduce-window.6
  13.0 0.2 slice_reduce_fusion
  13.3 1.4 scatter_custom_fusion
  14.8 2.5 gather_fusion
  17.3 0.7 all_to_all.25
  18.0 9.4 %all-to-all-start = ((bf16[32,1,10]{2,1,0:T(2,128)(2,1)}), bf16[32,1,10]{2,1,0:T(2,128)(2,1)S(1)}, u32[]{:S(2)}, u32[]{:S(2)}) async-start(bf16[32,1,10]{2,1,0:T(2,128)(2,1)} %all_to_all.25), calls=%async_computation | async-start | bytes 32768 | tf_op jit(solution)/shard_map/all_to_all | solution.py:35
  27.5 2.4 gather_fusion.2
  29.9 1.7 reshape.123
  31.6 1.1 all-to-all-done
  32.7 6.4 %all-to-all-start.2 = ((bf16[32,10,2048]{2,1,0:T(8,128)(2,1)}), bf16[32,10,2048]{2,1,0:T(8,128)(2,1)S(1)}, u32[]{:S(2)}, u32[]{:S(2)}) async-start(bf16[32,10,2048]{2,1,0:T(8,128)(2,1)} %reshape.123), calls=%async_computation.2 | async-start | bytes 4194304 | tf_op jit(solution)/shard_map/all_to_all | solution.py:33
  39.2 3.0 gather_fusion.1
  42.2 3.3 %reshape.122 = bf16[32,10,2048]{2,1,0:T(8,128)(2,1)} reshape(bf16[320,2048]{1,0:T(8,128)(2,1)} %gather_fusion.1) | data formatting | bytes 2621440 | tf_op jit(solution)/shard_map/reshape | solution.py:30
  45.6 19.5 %all-to-all-done.2 = bf16[32,10,2048]{2,1,0:T(8,128)(2,1)S(1)} async-done(((bf16[32,10,2048]{2,1,0:T(8,128)(2,1)}), bf16[32,10,2048]{2,1,0:T(8,128)(2,1)S(1)}, u32[]{:S(2)}, u32[]{:S(2)}) %all-to-all-start.2) | async-done | bytes 1310752 | tf_op jit(solution)/shard_map/all_to_all | solution.py:33
  65.0 7.7 %all-to-all-start.1 = ((bf16[32,10,2048]{2,1,0:T(8,128)(2,1)}), bf16[32,10,2048]{2,1,0:T(8,128)(2,1)}, u32[]{:S(2)}, u32[]{:S(2)}) async-start(bf16[32,10,2048]{2,1,0:T(8,128)(2,1)} %reshape.122), calls=%async_computation.1 | async-start | bytes 4194304 | tf_op jit(solution)/shard_map/all_to_all | solution.py:34
  72.7 0.2 reduce-scatter.2.cloned.1.call-start
  73.1 1.4 reshape.124
  74.5 24.1 %all-to-all-done.1 = bf16[32,10,2048]{2,1,0:T(8,128)(2,1)} async-done(((bf16[32,10,2048]{2,1,0:T(8,128)(2,1)}), bf16[32,10,2048]{2,1,0:T(8,128)(2,1)}, u32[]{:S(2)}, u32[]{:S(2)}) %all-to-all-start.1) | async-done | bytes 1310752 | tf_op jit(solution)/shard_map/all_to_all | solution.py:34
  98.6 2.5 reshape.130
  101.1 4.4 %fusion.2 = f32[320,768]{1,0:T(8,128)} fusion(bf16[320,2048]{1,0:T(8,128)(2,1)} %reshape.124, bf16[1,2048,768]{2,1,0:T(8,128)(2,1)} %all-gather.8.cloned.1.call-done), kind=kOutput, calls=%fused_computation.10 | convolution fusion | flops 1006632960 | bytes 5439488 | tf_op jit(solution)/shard_map/dot_general | solution.py:47
  105.6 58.7 %all-gather.6.cloned.1.call-done = bf16[1,2048,768]{2,1,0:T(8,128)(2,1)} async-done(((bf16[1,128,768]{2,1,0:T(8,128)(2,1)}), bf16[1,2048,768]{2,1,0:T(8,128)(2,1)}) %all-gather.6.cloned.1.call-update) | async-done | bytes 3145744 | tf_op jit(solution)/shard_map/all_gather | solution.py:43
  164.3 4.7 %multiply_convert_fusion.3 = (bf16[320,768]{1,0:T(8,128)(2,1)S(1)}, f32[320,768]{1,0:T(8,128)}) fusion(f32[320,768]{1,0:T(8,128)} %fusion.2, bf16[320,2048]{1,0:T(8,128)(2,1)} %reshape.124, bf16[1,2048,768]{2,1,0:T(8,128)(2,1)} %all-gather.6.cloned.1.call-done), kind=kOutput, calls=%fused_computation.26 | convolution fusion | flops 1008107520 | bytes 6914048 | tf_op jit(solution)/shard_map/dot_general | solution.py:48
  169.0 3.6 %convolution_convert_fusion = bf16[2048,768]{1,0:T(8,128)(2,1)} fusion(bf16[320,768]{1,0:T(8,128)(2,1)S(1)} %get-tuple-element.11, f32[320,2048]{1,0:T(8,128)S(1)} %reshape.130, f32[320]{0:T(512)S(1)} %reshape.131), kind=kOutput, calls=%fused_computation.7 | convolution fusion | flops 1009516544 | bytes 6259968 | tf_op jit(solution)/shard_map/dot_general | solution.py:66
  172.6 3.3 %multiply_convert_fusion = bf16[32,10,2048]{2,1,0:T(8,128)(2,1)} fusion(f32[32,10]{1,0:T(8,128)S(1)} %bitcast.54, bf16[32,10,2048]{2,1,0:T(8,128)(2,1)} %all-to-all-done.1), kind=kLoop, calls=%fused_computation.6 | loop fusion | flops 1966080 | bytes 2622720 | tf_op jit(solution)/shard_map/convert_element_type | solution.py:40
  175.9 3.6 %convert_element_type.80 = bf16[320,2048]{1,0:T(8,128)(2,1)} reshape(bf16[32,10,2048]{2,1,0:T(8,128)(2,1)} %multiply_convert_fusion) | data formatting | bytes 2621440 | tf_op jit(solution)/shard_map/convert_element_type | solution.py:40
  179.5 59.1 %all-gather.4.cloned.1.call-done = bf16[1,2048,768]{2,1,0:T(8,128)(2,1)} async-done(((bf16[1,128,768]{2,1,0:T(8,128)(2,1)}), bf16[1,2048,768]{2,1,0:T(8,128)(2,1)}) %all-gather.4.cloned.1.call-update) | async-done | bytes 3145744 | tf_op jit(solution)/shard_map/all_gather | solution.py:52
  238.7 3.2 fusion.21
  241.9 0.7 convert_element_type.96
  242.6 7.4 %all-to-all-start.4 = ((bf16[32,1,10]{2,1,0:T(2,128)(2,1)}), bf16[32,1,10]{2,1,0:T(2,128)(2,1)S(1)}, u32[]{:S(2)}, u32[]{:S(2)}) async-start(bf16[32,1,10]{2,1,0:T(2,128)(2,1)} %convert_element_type.96), calls=%async_computation.4 | async-start | bytes 32768 | tf_op jit(solution)/shard_map/all_to_all | solution.py:82
  250.1 3.6 %fusion.10 = f32[320,768]{1,0:T(8,128)S(1)} fusion(bf16[320,2048]{1,0:T(8,128)(2,1)} %convert_element_type.80, bf16[1,2048,768]{2,1,0:T(8,128)(2,1)} %all-gather.4.cloned.1.call-done), kind=kOutput, calls=%fused_computation.18 | convolution fusion | flops 1006632960 | bytes 5439488 | tf_op jit(solution)/shard_map/dot_general | solution.py:54
  253.8 1.3 fusion
  255.2 0.7 copy-done.3
  255.8 1.2 fusion.18
  257.0 1.6 reshape.125
  258.6 7.4 %all-to-all-start.3 = ((bf16[32,10,2048]{2,1,0:T(8,128)(2,1)}), bf16[32,10,2048]{2,1,0:T(8,128)(2,1)S(1)}, u32[]{:S(2)}, u32[]{:S(2)}) async-start(bf16[32,10,2048]{2,1,0:T(8,128)(2,1)} %reshape.125), calls=%async_computation.3 | async-start | bytes 4194304 | tf_op jit(solution)/shard_map/all_to_all | solution.py:75
  266.2 1.9 gather_fusion.4
  268.3 0.6 copy.23
  268.9 23.0 %all-to-all-done.3 = bf16[32,10,2048]{2,1,0:T(8,128)(2,1)S(1)} async-done(((bf16[32,10,2048]{2,1,0:T(8,128)(2,1)}), bf16[32,10,2048]{2,1,0:T(8,128)(2,1)S(1)}, u32[]{:S(2)}, u32[]{:S(2)}) %all-to-all-start.3) | async-done | bytes 1310752 | tf_op jit(solution)/shard_map/all_to_all | solution.py:75
  291.9 0.5 reshape.126
  292.4 1.4 gather_fusion.3
  293.8 0.7 gather.21
  294.5 3.6 %reduce_sum.34 = bf16[128,2048]{1,0:T(8,128)(2,1)} reduce(bf16[128,2,2048]{2,1,0:T(2,128)(2,1)S(1)} %gather.21, bf16[]{:T(256)} %constant.36.clone.1), dimensions={1}, to_apply=%region_4.5 | reduce | flops 262144 | bytes 1572866 | tf_op jit(solution)/shard_map/reduce_sum | solution.py:93
  298.1 17.8 %reduce-scatter.2.cloned.1.call-done = bf16[128,768]{1,0:T(8,128)(2,1)} async-done(((bf16[2048,768]{1,0:T(8,128)(2,1)}), bf16[128,768]{1,0:T(8,128)(2,1)}) %reduce-scatter.2.cloned.1.call-update) | async-done | bytes 196624 | tf_op jit(solution)/shard_map/reduce_scatter | solution.py:65
  (41 shorter events, 1.9 us)
Async XLA Ops:
  7.2 20.3 %copy-start = (bf16[128,2048]{1,0:T(8,128)(2,1)S(1)}, bf16[128,2048]{1,0:T(8,128)(2,1)}, u32[]{:S(2)}) copy-start(bf16[128,2048]{1,0:T(8,128)(2,1)} %param.7) | copy-start | bytes 1572868
  7.2 94.0 %all-gather.8.cloned.1.call-start = ((), (), s32[]{:S(2)}) async-start(), calls=%async_computation.8 | async-start | bytes 3342336 | tf_op jit(solution)/shard_map/all_gather | solution.py:42
  7.9 156.4 %all-gather.6.cloned.1.call-start = ((), (), s32[]{:S(2)}) async-start(), calls=%async_computation.7 | async-start | bytes 3342336 | tf_op jit(solution)/shard_map/all_gather | solution.py:43
  8.7 230.0 %all-gather.4.cloned.1.call-start = ((), (), s32[]{:S(2)}) async-start(), calls=%async_computation.6 | async-start | bytes 3342336 | tf_op jit(solution)/shard_map/all_gather | solution.py:52
  18.0 14.7 %all-to-all-start = ((bf16[32,1,10]{2,1,0:T(2,128)(2,1)}), bf16[32,1,10]{2,1,0:T(2,128)(2,1)S(1)}, u32[]{:S(2)}, u32[]{:S(2)}) async-start(bf16[32,1,10]{2,1,0:T(2,128)(2,1)} %all_to_all.25), calls=%async_computation | async-start | bytes 32768 | tf_op jit(solution)/shard_map/all_to_all | solution.py:35
  31.6 7.5 %copy-start.1 = (bf16[128,2048]{1,0:T(8,128)(2,1)S(1)}, bf16[128,2048]{1,0:T(8,128)(2,1)}, u32[]{:S(2)}) copy-start(bf16[128,2048]{1,0:T(8,128)(2,1)} %param.8) | copy-start | bytes 1572868
  32.7 32.4 %all-to-all-start.2 = ((bf16[32,10,2048]{2,1,0:T(8,128)(2,1)}), bf16[32,10,2048]{2,1,0:T(8,128)(2,1)S(1)}, u32[]{:S(2)}, u32[]{:S(2)}) async-start(bf16[32,10,2048]{2,1,0:T(8,128)(2,1)} %reshape.123), calls=%async_computation.2 | async-start | bytes 4194304 | tf_op jit(solution)/shard_map/all_to_all | solution.py:33
  65.0 33.6 %all-to-all-start.1 = ((bf16[32,10,2048]{2,1,0:T(8,128)(2,1)}), bf16[32,10,2048]{2,1,0:T(8,128)(2,1)}, u32[]{:S(2)}, u32[]{:S(2)}) async-start(bf16[32,10,2048]{2,1,0:T(8,128)(2,1)} %reshape.122), calls=%async_computation.1 | async-start | bytes 4194304 | tf_op jit(solution)/shard_map/all_to_all | solution.py:34
  72.7 243.2 %reduce-scatter.2.cloned.1.call-start = ((), (), s32[]{:S(2)}) async-start(), calls=%async_computation.9 | async-start | bytes 3342336 | tf_op jit(solution)/shard_map/reduce_scatter | solution.py:65
  242.6 16.0 %all-to-all-start.4 = ((bf16[32,1,10]{2,1,0:T(2,128)(2,1)}), bf16[32,1,10]{2,1,0:T(2,128)(2,1)S(1)}, u32[]{:S(2)}, u32[]{:S(2)}) async-start(bf16[32,1,10]{2,1,0:T(2,128)(2,1)} %convert_element_type.96), calls=%async_computation.4 | async-start | bytes 32768 | tf_op jit(solution)/shard_map/all_to_all | solution.py:82
  250.0 3.6 %copy-start.2 = (bf16[1,2048,768]{2,1,0:T(8,128)(2,1)S(1)}, bf16[1,2048,768]{2,1,0:T(8,128)(2,1)}, u32[]{:S(2)}) copy-start(bf16[1,2048,768]{2,1,0:T(8,128)(2,1)} %all-gather.8.cloned.1.call-done) | copy-start | bytes 9437188
  250.0 3.6 %copy-start.4 = (f32[320,768]{1,0:T(8,128)S(1)}, f32[320,768]{1,0:T(8,128)}, u32[]{:S(2)}) copy-start(f32[320,768]{1,0:T(8,128)} %fusion.2) | copy-start | bytes 2949124
  250.0 3.8 %copy-start.5 = (f32[320,768]{1,0:T(8,128)S(1)}, f32[320,768]{1,0:T(8,128)}, u32[]{:S(2)}) copy-start(f32[320,768]{1,0:T(8,128)} %get-tuple-element.12) | copy-start | bytes 2949124
  253.8 2.0 copy-start.3
  258.6 33.3 %all-to-all-start.3 = ((bf16[32,10,2048]{2,1,0:T(8,128)(2,1)}), bf16[32,10,2048]{2,1,0:T(8,128)(2,1)S(1)}, u32[]{:S(2)}, u32[]{:S(2)}) async-start(bf16[32,10,2048]{2,1,0:T(8,128)(2,1)} %reshape.125), calls=%async_computation.3 | async-start | bytes 4194304 | tf_op jit(solution)/shard_map/all_to_all | solution.py:75
Sparse Core Ops, SparseCore 0:
  10.1 79.8 all-gather.7
  92.0 72.2 all-gather.5
  166.4 72.2 all-gather.3
  241.9 73.9 reduce-scatter.1
where the time goes:
time: 323 us; the launch traced here: 322 us
  waiting for transfers between devices  205 us (63%)
  starting transfers between devices  38.7 us (12%)
  local copies, waits for them, and re-layouts  32.9 us (10%)
  matrix products  22.1 us (7%)
  between operations  14.1 us (4%)
  other arithmetic  9.22 us (3%)
    all_gather x1, waiting for transfers between devices, per_device(): piece_rows = lax.all_gather(w_down, 'dp', axis=1, tiled=True)[0]  59.1 us
    all_gather x1, waiting for transfers between devices, per_device(): lax.all_gather(w_up, 'dp', axis=1, tiled=True)  58.7 us
    all_to_all x1, waiting for transfers between devices, per_device(): lax.all_to_all(dy_slots, 'expert', split_axis=0, concat_axis=0, tiled=True)  24.1 us
    all_to_all x1, waiting for transfers between devices, per_device(): lax.all_to_all(x_grad.reshape(n_expert, capacity, model_width), 'expert',...  23 us
    all_to_all x1, waiting for transfers between devices, per_device(): lax.all_to_all(x_slots, 'expert', split_axis=0, concat_axis=0, tiled=True)  19.5 us
    reduce_scatter x1, waiting for transfers between devices, per_device(): lax.psum_scatter(lax.dot_general(scaled, hidden, (((0,), (0,)), ((), ()))...  17.8 us
    all_to_all x1, starting transfers between devices, per_device(): lax.all_to_all(p_slots, 'expert', split_axis=0, concat_axis=0, tiled=True)  9.43 us
    all_to_all x1, starting transfers between devices, per_device(): lax.all_to_all(dy_slots, 'expert', split_axis=0, concat_axis=0, tiled=True)  7.69 us
  transfers between devices with their start and end apart: 9, of which 7 were waited for; matrix products, arithmetic and copies ran while one was open for 19% of the time, Pallas kernels for 0%

commit v1 on v0

--- a/solution.py
+++ b/solution.py
@@ -2,6 +2,11 @@
 import jax.numpy as jnp
 from jax import lax
 from jax.sharding import PartitionSpec as P
+
+
+def tiled_gather(array, axis, dim):
+    copies = jnp.concatenate([array] * lax.axis_size(axis), axis=dim)
+    return lax.all_to_all(copies, axis, dim, dim, tiled=True)
 
 
 def per_device(x_tokens, grad_out, expert_ids, route_probs, w_gate, w_up, w_down):
@@ -49,7 +54,7 @@
     gate_sig = jax.nn.sigmoid(gate_pre)
     gate_act = gate_pre * gate_sig
     hidden = (gate_act * up_pre).astype(jnp.bfloat16)
-    piece_rows = lax.all_gather(w_down, "dp", axis=1, tiled=True)[0]
+    piece_rows = tiled_gather(w_down, "dp", 1)[0]
     out_piece = jnp.dot(hidden, piece_rows.T, preferred_element_type=jnp.float32)
     grad_sum = jnp.dot(scaled, piece_rows, preferred_element_type=jnp.float32)
     prob_sum = jnp.sum(dy_rows.astype(jnp.float32) * out_piece, axis=1)

time: 323 us -> 417 us (1.29)
  the two profiles are of different devices: /device:TPU:4 before, /device:TPU:1 now
where the time goes in v1:
time: 417 us; the launch traced here: 415 us
  waiting for transfers between devices  213 us (51%)
  local copies, waits for them, and re-layouts  71.4 us (17%)
  starting transfers between devices  50.6 us (12%)
  other arithmetic  42.4 us (10%)
  matrix products  24 us (6%)
  between operations  14.1 us (3%)
    all_gather x1, waiting for transfers between devices, per_device(): lax.all_gather(w_up, 'dp', axis=1, tiled=True)  163 us
    unnamed x1, other arithmetic  33.2 us
    unnamed x34, local copies, waits for them, and re-layouts  32.1 us
    all_to_all x1, waiting for transfers between devices, per_device(): lax.all_to_all(x_grad.reshape(n_expert, capacity, model_width), 'expert',...  25.4 us
    all_to_all x1, waiting for transfers between devices, per_device(): lax.all_to_all(x_slots, 'expert', split_axis=0, concat_axis=0, tiled=True)  20.8 us
    all_to_all x1, starting transfers between devices, tiled_gather(): return lax.all_to_all(copies, axis, dim, dim, tiled=True)  13.1 us
    all_to_all x1, starting transfers between devices, per_device(): lax.all_to_all(p_slots, 'expert', split_axis=0, concat_axis=0, tiled=True)  10.3 us
    all_to_all x1, starting transfers between devices, per_device(): lax.all_to_all(prob_sum.astype(jnp.bfloat16).reshape(n_expert, capacity),...  9.36 us
  transfers between devices with their start and end apart: 9, of which 4 were waited for; matrix products, arithmetic and copies ran while one was open for 33% of the time, Pallas kernels for 0%

profile of v1, /device:TPU:1, one launch (start us, length us, event | category | flops | bytes accessed | tf_op | source)
XLA Modules:
  0.0 415.2 jit_solution(840052673569704727)
XLA Ops:
  7.9 0.8 copy.66
  11.8 1.4 scatter_custom_fusion
  13.3 2.5 gather_fusion
  15.8 0.7 all_to_all.29
  16.5 10.3 %all-to-all-start = ((bf16[32,1,10]{2,1,0:T(2,128)(2,1)}), bf16[32,1,10]{2,1,0:T(2,128)(2,1)S(1)}, u32[]{:S(2)}, u32[]{:S(2)}) async-start(bf16[32,1,10]{2,1,0:T(2,128)(2,1)} %all_to_all.29), calls=%async_computation | async-start | bytes 32768 | tf_op jit(solution)/shard_map/all_to_all | solution.py:40
  26.8 1.1 concatenate.16
  27.9 2.4 gather_fusion.2
  30.4 1.6 reshape.123
  32.0 1.9 all-to-all-done
  33.8 5.7 %all-to-all-start.3 = ((bf16[32,10,2048]{2,1,0:T(8,128)(2,1)}), bf16[32,10,2048]{2,1,0:T(8,128)(2,1)}, u32[]{:S(2)}, u32[]{:S(2)}) async-start(bf16[32,10,2048]{2,1,0:T(8,128)(2,1)} %reshape.123), calls=%async_computation.3 | async-start | bytes 4194304 | tf_op jit(solution)/shard_map/all_to_all | solution.py:38
  39.6 2.4 gather_fusion.1
  42.1 1.6 reshape.122
  43.6 0.7 constant_dynamic-update-slice_fusion.15
  45.7 0.7 constant_dynamic-update-slice_fusion.12
  46.4 0.7 constant_dynamic-update-slice_fusion.11
  47.1 20.8 %all-to-all-done.3 = bf16[32,10,2048]{2,1,0:T(8,128)(2,1)} async-done(((bf16[32,10,2048]{2,1,0:T(8,128)(2,1)}), bf16[32,10,2048]{2,1,0:T(8,128)(2,1)}, u32[]{:S(2)}, u32[]{:S(2)}) %all-to-all-start.3) | async-done | bytes 1310752 | tf_op jit(solution)/shard_map/all_to_all | solution.py:38
  67.9 4.5 %all-to-all-start.1 = ((bf16[32,10,2048]{2,1,0:T(8,128)(2,1)}), bf16[32,10,2048]{2,1,0:T(8,128)(2,1)S(1)}, u32[]{:S(2)}, u32[]{:S(2)}) async-start(bf16[32,10,2048]{2,1,0:T(8,128)(2,1)} %reshape.122), calls=%async_computation.1 | async-start | bytes 4194304 | tf_op jit(solution)/shard_map/all_to_all | solution.py:39
  73.1 0.7 constant_dynamic-update-slice_fusion.9
  74.5 0.7 constant_dynamic-update-slice_fusion.7
  79.3 0.7 constant_dynamic-update-slice_fusion
  80.0 6.9 %copy.85 = bf16[1,2048,768]{2,0,1:T(2,128)(2,1)} copy(bf16[1,2048,768]{2,1,0:T(8,128)(2,1)} %constant_dynamic-update-slice_fusion) | data formatting | bytes 6291456 | tf_op jit(solution)/shard_map/concatenate | solution.py:8
  87.4 33.2 %reduce.8 = bf16[2048,768]{1,0:T(8,128)(2,1)} reduce(bf16[2048,1,768]{2,1,0:T(2,128)(2,1)} %bitcast.57, bf16[]{:T(256)} %broadcast.117), dimensions={1}, to_apply=%bitcast.56.reduce_sub_computation | reduce | bytes 6291458
  120.7 6.3 %reshape.194 = bf16[16,2,49152]{2,1,0:T(2,128)(2,1)} reshape(bf16[2048,768]{1,0:T(8,128)(2,1)} %reduce.8) | data formatting | bytes 6291456
  127.0 1.4 copy-done.1
  128.4 13.1 %all-to-all-start.2 = ((bf16[16,2,49152]{2,1,0:T(2,128)(2,1)}), bf16[16,2,49152]{2,1,0:T(2,128)(2,1)}, u32[]{:S(2)}, u32[]{:S(2)}) async-start(bf16[16,2,49152]{2,1,0:T(2,128)(2,1)} %reshape.194), calls=%async_computation.2 | async-start | bytes 6291456 | tf_op jit(solution)/shard_map/all_to_all | solution.py:9
  141.5 0.7 all-gather.3.cloned.1.call-update
  142.6 3.6 reshape.124
  146.2 2.5 reshape.130
  148.8 4.4 %fusion.6 = f32[320,768]{1,0:T(8,128)} fusion(bf16[320,2048]{1,0:T(8,128)(2,1)} %reshape.124, bf16[1,2048,768]{2,1,0:T(8,128)(2,1)} %all-gather.5.cloned.1.call-done), kind=kOutput, calls=%fused_computation.14 | convolution fusion | flops 1006632960 | bytes 5439488 | tf_op jit(solution)/shard_map/dot_general | solution.py:52
  153.2 163.1 %all-gather.3.cloned.1.call-done = bf16[1,2048,768]{2,1,0:T(8,128)(2,1)} async-done(((bf16[1,128,768]{2,1,0:T(8,128)(2,1)}), bf16[1,2048,768]{2,1,0:T(8,128)(2,1)}) %all-gather.3.cloned.1.call-update) | async-done | bytes 3145744 | tf_op jit(solution)/shard_map/all_gather | solution.py:48
  316.3 4.7 %multiply_convert_fusion.3 = (bf16[320,768]{1,0:T(8,128)(2,1)S(1)}, f32[320,768]{1,0:T(8,128)}) fusion(f32[320,768]{1,0:T(8,128)} %fusion.6, bf16[320,2048]{1,0:T(8,128)(2,1)} %reshape.124, bf16[1,2048,768]{2,1,0:T(8,128)(2,1)} %all-gather.3.cloned.1.call-done), kind=kOutput, calls=%fused_computation.28 | convolution fusion | flops 1008107520 | bytes 6914048 | tf_op jit(solution)/shard_map/dot_general | solution.py:53
  321.0 3.6 convolution_convert_fusion
  324.6 3.3 multiply_convert_fusion
  327.9 3.6 convert_element_type.80
  331.5 11.5 %reshape.195 = bf16[2048,1,768]{2,1,0:T(2,128)(2,1)} reshape(bf16[16,2,49152]{2,1,0:T(2,128)(2,1)} %all-to-all-done.2) | data formatting | bytes 6291456
  343.0 4.1 fusion.21
  347.1 0.7 convert_element_type.96
  347.9 9.4 %all-to-all-start.5 = ((bf16[32,1,10]{2,1,0:T(2,128)(2,1)}), bf16[32,1,10]{2,1,0:T(2,128)(2,1)S(1)}, u32[]{:S(2)}, u32[]{:S(2)}) async-start(bf16[32,1,10]{2,1,0:T(2,128)(2,1)} %convert_element_type.96), calls=%async_computation.5 | async-start | bytes 32768 | tf_op jit(solution)/shard_map/all_to_all | solution.py:87
  357.2 4.6 %fusion.2 = f32[320,768]{1,0:T(8,128)S(1)} fusion(bf16[320,2048]{1,0:T(8,128)(2,1)} %convert_element_type.80, bf16[1,2048,768]{2,0,1:T(2,128)(2,1)} %bitcast.59), kind=kOutput, calls=%fused_computation.10 | convolution fusion | flops 1006632960 | bytes 5439488 | tf_op jit(solution)/shard_map/dot_general | solution.py:59
  361.9 1.3 fusion.4
  363.9 1.2 fusion.18
  365.1 1.6 reshape.125
  366.7 7.4 %all-to-all-start.4 = ((bf16[32,10,2048]{2,1,0:T(8,128)(2,1)}), bf16[32,10,2048]{2,1,0:T(8,128)(2,1)S(1)}, u32[]{:S(2)}, u32[]{:S(2)}) async-start(bf16[32,10,2048]{2,1,0:T(8,128)(2,1)} %reshape.125), calls=%async_computation.4 | async-start | bytes 4194304 | tf_op jit(solution)/shard_map/all_to_all | solution.py:80
  374.3 1.9 gather_fusion.4
  377.0 25.4 %all-to-all-done.4 = bf16[32,10,2048]{2,1,0:T(8,128)(2,1)S(1)} async-done(((bf16[32,10,2048]{2,1,0:T(8,128)(2,1)}), bf16[32,10,2048]{2,1,0:T(8,128)(2,1)S(1)}, u32[]{:S(2)}, u32[]{:S(2)}) %all-to-all-start.4) | async-done | bytes 1310752 | tf_op jit(solution)/shard_map/all_to_all | solution.py:80
  402.9 1.4 gather_fusion.3
  404.3 0.7 gather.21
  405.0 3.6 reduce_sum.34
  (63 shorter events, 13.9 us)
Async XLA Ops:
  7.2 141.6 %all-gather.5.cloned.1.call-start = ((), (), s32[]{:S(2)}) async-start(), calls=%async_computation.8 | async-start | bytes 3342336 | tf_op jit(solution)/shard_map/all_gather | solution.py:47
  16.5 17.3 %all-to-all-start = ((bf16[32,1,10]{2,1,0:T(2,128)(2,1)}), bf16[32,1,10]{2,1,0:T(2,128)(2,1)S(1)}, u32[]{:S(2)}, u32[]{:S(2)}) async-start(bf16[32,1,10]{2,1,0:T(2,128)(2,1)} %all_to_all.29), calls=%async_computation | async-start | bytes 32768 | tf_op jit(solution)/shard_map/all_to_all | solution.py:40
  30.3 9.2 %copy-start.2 = (bf16[128,2048]{1,0:T(8,128)(2,1)S(1)}, bf16[128,2048]{1,0:T(8,128)(2,1)}, u32[]{:S(2)}) copy-start(bf16[128,2048]{1,0:T(8,128)(2,1)} %param.8) | copy-start | bytes 1572868
  33.8 34.1 %all-to-all-start.3 = ((bf16[32,10,2048]{2,1,0:T(8,128)(2,1)}), bf16[32,10,2048]{2,1,0:T(8,128)(2,1)}, u32[]{:S(2)}, u32[]{:S(2)}) async-start(bf16[32,10,2048]{2,1,0:T(8,128)(2,1)} %reshape.123), calls=%async_computation.3 | async-start | bytes 4194304 | tf_op jit(solution)/shard_map/all_to_all | solution.py:38
  42.0 1.6 copy-start
  67.9 59.1 %all-to-all-start.1 = ((bf16[32,10,2048]{2,1,0:T(8,128)(2,1)}), bf16[32,10,2048]{2,1,0:T(8,128)(2,1)S(1)}, u32[]{:S(2)}, u32[]{:S(2)}) async-start(bf16[32,10,2048]{2,1,0:T(8,128)(2,1)} %reshape.122), calls=%async_computation.1 | async-start | bytes 4194304 | tf_op jit(solution)/shard_map/all_to_all | solution.py:39
  127.0 1.4 copy-start.1
  128.4 203.1 %all-to-all-start.2 = ((bf16[16,2,49152]{2,1,0:T(2,128)(2,1)}), bf16[16,2,49152]{2,1,0:T(2,128)(2,1)}, u32[]{:S(2)}, u32[]{:S(2)}) async-start(bf16[16,2,49152]{2,1,0:T(2,128)(2,1)} %reshape.194), calls=%async_computation.2 | async-start | bytes 6291456 | tf_op jit(solution)/shard_map/all_to_all | solution.py:9
  141.5 174.8 %all-gather.3.cloned.1.call-start = ((), (), s32[]{:S(2)}) async-start(), calls=%async_computation.7 | async-start | bytes 3342336 | tf_op jit(solution)/shard_map/all_gather | solution.py:48
  142.2 266.4 %reduce-scatter.2.cloned.1.call-start = ((), (), s32[]{:S(2)}) async-start(), calls=%async_computation.9 | async-start | bytes 3342336 | tf_op jit(solution)/shard_map/reduce_scatter | solution.py:70
  347.9 18.8 %all-to-all-start.5 = ((bf16[32,1,10]{2,1,0:T(2,128)(2,1)}), bf16[32,1,10]{2,1,0:T(2,128)(2,1)S(1)}, u32[]{:S(2)}, u32[]{:S(2)}) async-start(bf16[32,1,10]{2,1,0:T(2,128)(2,1)} %convert_element_type.96), calls=%async_computation.5 | async-start | bytes 32768 | tf_op jit(solution)/shard_map/all_to_all | solution.py:87
  357.2 4.6 %copy-start.3 = (bf16[1,2048,768]{2,1,0:T(8,128)(2,1)S(1)}, bf16[1,2048,768]{2,1,0:T(8,128)(2,1)}, u32[]{:S(2)}) copy-start(bf16[1,2048,768]{2,1,0:T(8,128)(2,1)} %all-gather.5.cloned.1.call-done) | copy-start | bytes 9437188
  357.2 4.6 %copy-start.5 = (f32[320,768]{1,0:T(8,128)S(1)}, f32[320,768]{1,0:T(8,128)}, u32[]{:S(2)}) copy-start(f32[320,768]{1,0:T(8,128)} %fusion.6) | copy-start | bytes 2949124
  357.2 4.7 %copy-start.6 = (f32[320,768]{1,0:T(8,128)S(1)}, f32[320,768]{1,0:T(8,128)}, u32[]{:S(2)}) copy-start(f32[320,768]{1,0:T(8,128)} %get-tuple-element.18) | copy-start | bytes 2949124
  361.9 1.9 copy-start.4
  366.7 35.7 %all-to-all-start.4 = ((bf16[32,10,2048]{2,1,0:T(8,128)(2,1)}), bf16[32,10,2048]{2,1,0:T(8,128)(2,1)S(1)}, u32[]{:S(2)}, u32[]{:S(2)}) async-start(bf16[32,10,2048]{2,1,0:T(8,128)(2,1)} %reshape.125), calls=%async_computation.4 | async-start | bytes 4194304 | tf_op jit(solution)/shard_map/all_to_all | solution.py:80
Sparse Core Ops, SparseCore 0:
  10.0 72.0 all-gather.4
  144.4 171.8 all-gather.2
  324.7 67.8 reduce-scatter.1
